TPU v7x, 512 devices: a whole 4x4x16 slice. The times are simulated.
512 devices in a mesh: gx: 16 (over y, z_hi, core), gy: 32 (over z_lo, x).
Axes of the slice: x: 4, y: 4, z: 16 (z_hi: 2, z_lo: 8; z = z_hi * 8 + z_lo), core: 2. Of those that a mesh axis runs over, the one named last changes fastest.
Arguments:
- layer_input: bfloat16 [16384, 2048], P('gy', 'gx'), may hold values from -6 to 6
- project_weight: bfloat16 [2048, 3, 2048], P(None, None, 'gx'), may hold values from -0.125 to 0.125
- output_weight: bfloat16 [2048, 2048], P('gx'), may hold values from -0.5 to 0.5
- cache_entries: bfloat16 [32, 3584, 2, 2048], P('gy', None, None, 'gx'), may hold values from -400 to 400, as said below
- cached_lengths: int32 [32], replicated, may hold values from 1 to 3584, as said below
- final_gain: bfloat16 [2048], P('gx'), may hold values from 0.099609375 to 1.8984375
- head_weight: bfloat16 [76032, 2048], P('gy', 'gx'), may hold values from -0.125 to 0.125
Outputs:
- layer_output: bfloat16 [16384, 2048], P('gy', 'gx')
- appended_entries: bfloat16 [16384, 2, 2048], P('gy', None, 'gx')
- logit_scale: float32 [32], P('gx')
- logit_peak: float32 [32], P('gx')
Inputs may be any that keep to these rules, and one draw needn't show every extreme that they name: `cached_lengths`: every request has one cached slot or more; in every draw one request uses all 3584 slots and another exactly one. `cache_entries`: slots at or beyond a request's cached length are never read.
All inputs are finite; a program needn't handle non-finite values.
Results may differ from a plain program's by a relative error of at most 0.015.
Values may be sent and summed in bfloat16 or wider, within the bound.
No kernel may reach another device: no remote copies, remote signals or barrier semaphores. Data moves between devices by JAX's collectives and lax.ppermute only.
A program may use at most 64 MiB of HBM per device.

v0:
```python
import jax
import jax.numpy as jnp
from jax import lax
from jax.sharding import PartitionSpec as P

D = 2048
HEAD_DIM = 128
VOCAB = 76032
NEG_FILL = -1e30


def combined_all(part, axis, combine):
    gathered = jax.tree.map(lambda a: lax.all_gather(a, axis), part)

    def take(source):
        return jax.tree.map(lambda a: lax.dynamic_index_in_dim(a, source, 0, False), gathered)

    return lax.fori_loop(
        1, lax.axis_size(axis), lambda source, state: combine(state, take(source)), take(0)
    )


def fold_scores(carried, queries, key_block, value_block, allowed):
    running_max, mass_sum, weighted = carried
    scores = jnp.einsum(
        "qhd,khd->hqk", queries, key_block, preferred_element_type=jnp.float32
    ) * HEAD_DIM ** (-0.5)
    scores = jnp.where(allowed, scores, NEG_FILL)
    new_max = jnp.maximum(running_max, jnp.max(scores, axis=2))
    weights = jnp.where(allowed, jnp.exp(scores - new_max[:, :, None]), 0.0)
    factor = jnp.exp(running_max - new_max)
    mass_sum = mass_sum * factor + jnp.sum(weights, axis=2)
    weighted = weighted * factor[:, :, None] + jnp.einsum(
        "hqk,khd->hqd", weights, value_block.astype(jnp.float32), precision=lax.Precision.HIGHEST
    )
    return (new_max, mass_sum, weighted)


def cache_pass(queries, cache_part, live_slots, block_rows):
    query_rows, head_count, head_width = queries.shape
    block_count = cache_part.shape[0] // block_rows
    live_slots = jnp.clip(live_slots, 0, cache_part.shape[0])
    initial = (
        jnp.full((head_count, query_rows), NEG_FILL, jnp.float32),
        jnp.zeros((head_count, query_rows), jnp.float32),
        jnp.zeros((head_count, query_rows, head_width), jnp.float32),
    )

    def advance(block_index, carried):
        cache_piece = lax.dynamic_slice_in_dim(cache_part, block_index * block_rows, block_rows, 0)
        key_block = cache_piece[:, 0].reshape(block_rows, head_count, head_width)
        value_block = cache_piece[:, 1].reshape(block_rows, head_count, head_width)
        places = block_index * block_rows + jnp.arange(block_rows, dtype=jnp.int32)
        allowed = (places < live_slots)[None, None, :]
        return fold_scores(carried, queries, key_block, value_block, allowed)

    return lax.fori_loop(0, block_count, advance, initial)


def combine_stats(earlier, other_side):
    return (earlier[0] + other_side[0], jnp.maximum(earlier[1], other_side[1]))


def per_device(
    layer_input,
    project_weight,
    output_weight,
    cache_entries,
    cached_lengths,
    final_gain,
    head_weight,
):
    new_rows = layer_input.shape[0]
    head_count = output_weight.shape[0] // HEAD_DIM
    request = lax.axis_index("gy")
    own_len = lax.dynamic_index_in_dim(cached_lengths, request, 0, keepdims=False)
    features = lax.all_gather(layer_input, "gx", axis=1, tiled=True)
    widened = features.astype(jnp.float32)
    normed = (
        widened * lax.rsqrt(jnp.mean(widened * widened, axis=1, keepdims=True) + 1e-06)
    ).astype(jnp.bfloat16)
    projected = jnp.einsum(
        "td,dcf->tcf", normed, project_weight, preferred_element_type=jnp.float32
    )
    rounded = projected.astype(jnp.bfloat16)
    queries = rounded[:, 0].reshape(new_rows, head_count, HEAD_DIM)
    new_keys = rounded[:, 1].reshape(new_rows, head_count, HEAD_DIM)
    new_values = rounded[:, 2].reshape(new_rows, head_count, HEAD_DIM)
    appended = rounded[:, 1:3]
    cache_local = cache_entries[0]
    cache_slots = cache_local.shape[0]
    block_rows = min(256, cache_slots // 2)
    carried = cache_pass(queries, cache_local, own_len, block_rows)
    causal = (jnp.arange(new_rows)[None, :] <= jnp.arange(new_rows)[:, None])[None]
    carried = fold_scores(carried, queries, new_keys, new_values, causal)
    attended = (carried[2] / carried[1][:, :, None]).astype(jnp.bfloat16)
    attended = jnp.transpose(attended, (1, 0, 2)).reshape(new_rows, head_count * HEAD_DIM)
    partial_out = jnp.dot(attended, output_weight, preferred_element_type=jnp.float32)
    branch_sum = lax.psum_scatter(
        partial_out.astype(jnp.bfloat16), "gx", scatter_dimension=1, tiled=True
    ).astype(jnp.float32)
    layer_output = (layer_input.astype(jnp.float32) + branch_sum).astype(jnp.bfloat16)
    last_row = layer_output[new_rows - 1 :]
    every_last = lax.all_gather(last_row, "gy", axis=0, tiled=True)
    last_wide = every_last.astype(jnp.float32)
    square_part = jnp.sum(last_wide * last_wide, axis=1)
    gained = (last_wide * final_gain.astype(jnp.float32)).astype(jnp.bfloat16)
    logit_part = jnp.einsum("rd,vd->rv", gained, head_weight, preferred_element_type=jnp.float32)
    logit_rows, square_rows = (
        lax.psum_scatter(logit_part, "gx", scatter_dimension=0, tiled=True),
        lax.psum_scatter(square_part, "gx", scatter_dimension=0, tiled=True),
    )
    logits = logit_rows * lax.rsqrt(square_rows / D + 1e-06)[:, None]
    square_sums = jnp.sum(logits * logits, axis=1)
    row_peaks = jnp.max(logits, axis=1)
    total_squares, logit_peak = combined_all((square_sums, row_peaks), "gy", combine_stats)
    logit_scale = jnp.sqrt(total_squares / VOCAB)
    return (layer_output, appended, logit_scale, logit_peak)


def solution(mesh):
    return jax.shard_map(
        per_device,
        mesh=mesh,
        in_specs=(
            P("gy", "gx"),
            P(None, None, "gx"),
            P("gx", None),
            P("gy", None, None, "gx"),
            P(),
            P("gx"),
            P("gy", "gx"),
        ),
        out_specs=(P("gy", "gx"), P("gy", None, "gx"), P("gx"), P("gx")),
        check_vma=False,
    )
```

profile of v0, /device:TPU:0, one launch (start us, length us, event | category | flops | bytes accessed | tf_op | source)
XLA Modules:
  0.0 776.4 jit_solution(6854591349324929596)
XLA Ops:
  8.0 3.0 copy.20
  12.2 88.2 %all-gather.5.cloned.1.call-done = bf16[512,2048]{1,0:T(8,128)(2,1)} async-done(((bf16[512,128]{1,0:T(8,128)(2,1)}), bf16[512,2048]{1,0:T(8,128)(2,1)}) %all-gather.5.cloned.1.call-update) | async-done | bytes 2097168 | tf_op jit(solution)/shard_map/all_gather | solution.py:77
  100.4 2.2 fusion.13
  102.6 1.3 fusion.20
  104.0 0.9 fusion.39
  104.9 57.1 %while.36 = (s32[]{:T(128)}, f32[1,512]{1,0:T(1,128)S(1)}, f32[1,512]{1,0:T(1,128)}, f32[1,512,128]{2,1,0:T(8,128)S(1)}, s32[]{:T(128)}, /*index=5*/bf16[3584,2,...) while((s32[]{:T(128)}, f32[1,512]{1,0:T(1,128)S(1)}, ...), condition=%wide.region_4.5_spmd.clone, body=%wide.region_1.4_spmd.clone.sunk | while | flops 236129280 | bytes 2393295 | solution.py:57
  104.9 1.1 fusion.49
  106.7 1.6 fusion.53
  108.3 1.1 fusion.49
  109.6 1.3 fusion.52
  110.8 1.6 fusion.53
  112.5 1.1 fusion.49
  113.7 1.3 fusion.52
  115.0 1.6 fusion.53
  116.6 1.1 fusion.49
  117.8 1.3 fusion.52
  119.1 1.6 fusion.53
  120.7 1.1 fusion.49
  122.0 1.3 fusion.52
  123.2 1.6 fusion.53
  124.9 1.1 fusion.49
  126.1 1.3 fusion.52
  127.4 1.6 fusion.53
  129.0 1.1 fusion.49
  130.2 1.3 fusion.52
  131.5 1.6 fusion.53
  133.1 1.1 fusion.49
  134.4 1.3 fusion.52
  135.6 1.6 fusion.53
  137.2 1.1 fusion.49
  138.5 1.3 fusion.52
  139.8 1.6 fusion.53
  141.4 1.1 fusion.49
  142.6 1.3 fusion.52
  143.9 1.6 fusion.53
  145.5 1.1 fusion.49
  146.7 1.3 fusion.52
  148.0 1.6 fusion.53
  149.6 1.1 fusion.49
  150.9 1.3 fusion.52
  152.2 1.6 fusion.53
  153.8 1.1 fusion.49
  155.0 1.3 fusion.52
  156.3 1.6 fusion.53
  157.9 1.1 fusion.49
  159.1 1.3 fusion.52
  160.4 1.6 fusion.53
  162.0 0.7 max.26
  162.9 0.7 multiply_add_fusion
  163.6 1.7 fusion.26
  165.3 2.0 convolution_convert_fusion
  167.3 3.9 copy.17
  171.9 112.6 %reduce-scatter.4.cloned.1.call-done = bf16[128,512]{1,0:T(8,128)(2,1)} async-done(((bf16[2048,512]{1,0:T(8,128)(2,1)}), bf16[128,512]{1,0:T(8,128)(2,1)}) %reduce-scatter.4.cloned.1.call-update) | async-done | bytes 131088
  284.5 1.0 copy.18
  285.7 112.4 %all-gather.2 = bf16[32,1,128]{2,1,0:T(2,128)(2,1)S(1)} all-gather(bf16[1,1,128]{2,1,0:T(2,128)(2,1)S(1)} %slice_bitcast_fusion.4), channel_id=1, replica_groups=mesh['gx'=16,'gy'=32] {'gy'}, dimensions={0}, use_global_device_ids=true | all-gather | bytes 8448 | tf_op jit(solution)/shard_map/all_gather | solution.py:104
  398.1 1.0 fusion.32
  399.1 1.3 dynamic-slice.2
  401.1 1.3 dynamic-slice
  403.0 1.0 copy.16
  404.1 62.1 %all-reduce.3 = f32[32]{0:T(128)S(1)} all-reduce(f32[32]{0:T(128)S(1)} %multiply_reduce_fusion.1), channel_id=6, replica_groups=mesh['gx'=16,'gy'=32] {'gx'}, use_global_device_ids=true, to_apply=%region_10.11.clone | all-reduce | flops 32 | bytes 256
  466.2 177.4 %all-reduce.7.cloned.1.call-done = f32[32,2376]{1,0:T(8,128)} async-done(((f32[32,2376]{1,0:T(8,128)}), f32[32,2376]{1,0:T(8,128)}) %all-reduce.7.cloned.1.call-update) | async-done | bytes 304144
  643.7 1.1 fusion.31
  645.3 122.6 %all-reduce.4 = (f32[64]{0:T(128)S(1)}, f32[64]{0:T(128)S(1)}) all-reduce(f32[64]{0:T(128)S(1)} %dynamic-update-slice, f32[64]{0:T(128)S(1)} %dynamic-update-slice.1), channel_id=2, replica_groups=mesh['gx'=16,'gy'=32] {'gy'}, use_global_device_ids=true, to_apply=%add | all-reduce | flops 128 | bytes 1024
  768.0 1.3 while.35
  (136 shorter events, 6.8 us)
Async XLA Ops:
  7.2 95.5 %copy-start = (bf16[2048,3,128]{2,0,1:T(8,128)(2,1)S(1)}, bf16[2048,3,128]{2,0,1:T(8,128)(2,1)}, u32[]{:S(2)}) copy-start(bf16[2048,3,128]{2,0,1:T(8,128)(2,1)} %param.12) | copy-start | bytes 4718596
  7.2 3.8 copy-start.8
  7.2 93.2 %all-gather.5.cloned.1.call-start = ((), (), s32[]{:S(2)}) async-start(), calls=%async_computation.1 | async-start | bytes 2228224 | tf_op jit(solution)/shard_map/all_gather | solution.py:77
  7.9 276.6 %reduce-scatter.4.cloned.1.call-start = ((), (), s32[]{:S(2)}) async-start(), calls=%async_computation.2 | async-start | bytes 2228224
  100.4 2.2 copy-start.1
  103.9 0.9 copy-start.2
  162.0 3.3 copy-start.5
  171.2 0.7 copy-start.9
  171.2 114.3 %copy-start.4 = (bf16[512,128]{1,0:T(8,128)(2,1)S(1)}, bf16[512,128]{1,0:T(8,128)(2,1)}, u32[]{:S(2)}) copy-start(bf16[512,128]{1,0:T(8,128)(2,1)} %param.11) | copy-start | bytes 393220
  171.2 226.8 %copy-start.3 = (bf16[2376,128]{1,0:T(8,128)(2,1)S(1)}, bf16[2376,128]{1,0:T(8,128)(2,1)}, u32[]{:S(2)}) copy-start(bf16[2376,128]{1,0:T(8,128)(2,1)} %param.17) | copy-start | bytes 1824772
  171.2 231.7 %slice-start = ((bf16[512,3,128]{2,0,1:T(8,128)(2,1)}), bf16[512,2,128]{2,0,1:T(8,128)(2,1)S(1)}, s32[]{:S(2)}) async-start(bf16[512,3,128]{2,0,1:T(8,128)(2,1)} %copy-done.2), calls=%async_computation.4 | async-start | bytes 524288 | tf_op jit(solution)/shard_map/slice | solution.py:89
  171.3 472.4 %all-reduce.7.cloned.1.call-start = ((), (), s32[]{:S(2)}) async-start(), calls=%async_computation.3 | async-start | bytes 622592
  285.6 484.3 %copy-start.6 = (bf16[512,128]{1,0:T(8,128)(2,1)}, bf16[512,128]{1,0:T(8,128)(2,1)S(1)}, u32[]{:S(2)}) copy-start(bf16[512,128]{1,0:T(8,128)(2,1)S(1)} %add_convert_fusion) | copy-start | bytes 393220
  769.4 0.5 copy-start.7
Sparse Core Ops, SparseCore 0:
  11.2 89.1 all-gather.4
  171.4 113.0 reduce-scatter.3
  399.2 244.3 all-reduce.6
where the time goes:
time: 778 us; the launch traced here: 776 us
  waiting for transfers between devices  379 us (49%)
  blocking collectives  297 us (38%)
  matrix products  44 us (6%)
  other arithmetic  25.5 us (3%)
  between operations  15.9 us (2%)
  local copies, waits for them, and re-layouts  13.4 us (2%)
    unnamed x5, waiting for transfers between devices  291 us
    unnamed x2, blocking collectives  185 us
    all_gather x1, blocking collectives, per_device(): every_last = lax.all_gather(last_row, 'gy', axis=0, tiled=True)  112 us
    all_gather x1, waiting for transfers between devices, per_device(): features = lax.all_gather(layer_input, 'gx', axis=1, tiled=True)  88.2 us
    dot_general x15, matrix products, fold_scores(): jnp.einsum('hqk,khd->hqd', weights, value_block.astype(jnp.float32), prec...  23.6 us
    add x15, other arithmetic, fold_scores(): mass_sum = mass_sum * factor + jnp.sum(weights, axis=2)  17.9 us
    dot_general x15, matrix products, fold_scores(): jnp.einsum('qhd,khd->hqk', queries, key_block, preferred_element_type=jnp...  16.1 us
  transfers between devices with their start and end apart: 3, of which 3 were waited for; matrix products, arithmetic and copies ran while one was open for 1% of the time, Pallas kernels for 0%

commit v1 on v0

--- a/solution.py
+++ b/solution.py
@@ -101,7 +101,10 @@
     ).astype(jnp.float32)
     layer_output = (layer_input.astype(jnp.float32) + branch_sum).astype(jnp.bfloat16)
     last_row = layer_output[new_rows - 1 :]
-    every_last = lax.all_gather(last_row, "gy", axis=0, tiled=True)
+    devices = lax.axis_size("gy")
+    blocks = jnp.stack([last_row for _ in range(devices)])
+    blocks = lax.all_to_all(blocks, "gy", split_axis=0, concat_axis=0)
+    every_last = jnp.concatenate(blocks, axis=0)
     last_wide = every_last.astype(jnp.float32)
     square_part = jnp.sum(last_wide * last_wide, axis=1)
     gained = (last_wide * final_gain.astype(jnp.float32)).astype(jnp.bfloat16)

time: 778 us -> 686 us (0.88)
  blocking collectives: 297 us -> 189 us
  waiting for transfers between devices: 379 us -> 389 us
    all_gather x1 -> x0, blocking collectives: 112 us -> none  [per_device(): every_last = lax.all_gather(last_row, 'gy', axis=0, tiled=True)]
    all_to_all x0 -> x1, waiting for transfers between devices: none -> 12.4 us  [per_device(): blocks = lax.all_to_all(blocks, 'gy', split_axis=0, concat_axis=0)]
  transfers between devices with their start and end apart: 3 -> 4, of which waited for: 3 -> 4; matrix products, arithmetic and copies ran while one was open for 1% -> 1% of each run, Pallas kernels for 0% -> 0%
where the time goes in v1:
time: 686 us; the launch traced here: 684 us
  waiting for transfers between devices  389 us (57%)
  blocking collectives  189 us (28%)
  matrix products  44 us (6%)
  other arithmetic  25.5 us (4%)
  between operations  16 us (2%)
  local copies, waits for them, and re-layouts  13.4 us (2%)
    unnamed x5, waiting for transfers between devices  289 us
    unnamed x2, blocking collectives  189 us
    all_gather x1, waiting for transfers between devices, per_device(): features = lax.all_gather(layer_input, 'gx', axis=1, tiled=True)  88.2 us
    dot_general x15, matrix products, fold_scores(): jnp.einsum('hqk,khd->hqd', weights, value_block.astype(jnp.float32), prec...  23.6 us
    add x15, other arithmetic, fold_scores(): mass_sum = mass_sum * factor + jnp.sum(weights, axis=2)  17.9 us
    dot_general x15, matrix products, fold_scores(): jnp.einsum('qhd,khd->hqk', queries, key_block, preferred_element_type=jnp...  16.1 us
  transfers between devices with their start and end apart: 4, of which 4 were waited for; matrix products, arithmetic and copies ran while one was open for 1% of the time, Pallas kernels for 0%

profile of v1, /device:TPU:0, one launch (start us, length us, event | category | flops | bytes accessed | tf_op | source)
XLA Modules:
  0.0 683.8 jit_solution(18303286564782547247)
XLA Ops:
  8.0 3.0 copy.24
  12.2 88.2 %all-gather.4.cloned.1.call-done = bf16[512,2048]{1,0:T(8,128)(2,1)} async-done(((bf16[512,128]{1,0:T(8,128)(2,1)}), bf16[512,2048]{1,0:T(8,128)(2,1)}) %all-gather.4.cloned.1.call-update) | async-done | bytes 2097168 | tf_op jit(solution)/shard_map/all_gather | solution.py:77
  100.4 2.2 fusion.13
  102.6 1.3 fusion.20
  104.0 0.9 fusion.39
  104.9 57.1 %while.36 = (s32[]{:T(128)}, f32[1,512]{1,0:T(1,128)S(1)}, f32[1,512]{1,0:T(1,128)}, f32[1,512,128]{2,1,0:T(8,128)S(1)}, s32[]{:T(128)}, /*index=5*/bf16[3584,2,...) while((s32[]{:T(128)}, f32[1,512]{1,0:T(1,128)S(1)}, ...), condition=%wide.region_4.5_spmd.clone, body=%wide.region_1.4_spmd.clone.sunk | while | flops 236129280 | bytes 2393295 | solution.py:57
  104.9 1.1 fusion.49
  106.7 1.6 fusion.53
  108.3 1.1 fusion.49
  109.6 1.3 fusion.52
  110.8 1.6 fusion.53
  112.5 1.1 fusion.49
  113.7 1.3 fusion.52
  115.0 1.6 fusion.53
  116.6 1.1 fusion.49
  117.8 1.3 fusion.52
  119.1 1.6 fusion.53
  120.7 1.1 fusion.49
  122.0 1.3 fusion.52
  123.2 1.6 fusion.53
  124.9 1.1 fusion.49
  126.1 1.3 fusion.52
  127.4 1.6 fusion.53
  129.0 1.1 fusion.49
  130.2 1.3 fusion.52
  131.5 1.6 fusion.53
  133.1 1.1 fusion.49
  134.4 1.3 fusion.52
  135.6 1.6 fusion.53
  137.2 1.1 fusion.49
  138.5 1.3 fusion.52
  139.8 1.6 fusion.53
  141.4 1.1 fusion.49
  142.6 1.3 fusion.52
  143.9 1.6 fusion.53
  145.5 1.1 fusion.49
  146.7 1.3 fusion.52
  148.0 1.6 fusion.53
  149.6 1.1 fusion.49
  150.9 1.3 fusion.52
  152.2 1.6 fusion.53
  153.8 1.1 fusion.49
  155.0 1.3 fusion.52
  156.3 1.6 fusion.53
  157.9 1.1 fusion.49
  159.1 1.3 fusion.52
  160.4 1.6 fusion.53
  162.0 0.7 max.26
  163.6 1.7 fusion.26
  165.3 2.0 convolution_convert_fusion
  167.3 3.9 copy.21
  171.3 113.3 %reduce-scatter.4.cloned.1.call-done = bf16[128,512]{1,0:T(8,128)(2,1)} async-done(((bf16[2048,512]{1,0:T(8,128)(2,1)}), bf16[128,512]{1,0:T(8,128)(2,1)}) %reduce-scatter.4.cloned.1.call-update) | async-done | bytes 131088
  284.5 1.0 copy.22
  286.3 4.9 all-to-all-start
  291.3 12.4 %all-to-all-done = bf16[32,1,128]{2,1,0:T(2,128)(2,1)S(1)} async-done(((bf16[32,1,128]{2,1,0:T(2,128)(2,1)}), bf16[32,1,128]{2,1,0:T(2,128)(2,1)S(1)}, u32[]{:S(2)}, u32[]{:S(2)}) %all-to-all-start) | async-done | bytes 8224 | tf_op jit(solution)/shard_map/all_to_all | solution.py:106
  303.7 1.0 fusion.32
  304.8 1.3 dynamic-slice.2
  306.7 1.3 dynamic-slice
  308.7 1.0 copy.20
  309.7 66.6 %all-reduce.3 = f32[32]{0:T(128)S(1)} all-reduce(f32[32]{0:T(128)S(1)} %multiply_reduce_fusion.1), channel_id=6, replica_groups=mesh['gx'=16,'gy'=32] {'gx'}, use_global_device_ids=true, to_apply=%region_10.11.clone | all-reduce | flops 32 | bytes 256
  376.4 174.6 %all-reduce.7.cloned.1.call-done = f32[32,2376]{1,0:T(8,128)} async-done(((f32[32,2376]{1,0:T(8,128)}), f32[32,2376]{1,0:T(8,128)}) %all-reduce.7.cloned.1.call-update) | async-done | bytes 304144
  551.1 1.1 fusion.31
  552.6 122.6 %all-reduce.4 = (f32[64]{0:T(128)S(1)}, f32[64]{0:T(128)S(1)}) all-reduce(f32[64]{0:T(128)S(1)} %dynamic-update-slice, f32[64]{0:T(128)S(1)} %dynamic-update-slice.1), channel_id=2, replica_groups=mesh['gx'=16,'gy'=32] {'gy'}, use_global_device_ids=true, to_apply=%add | all-reduce | flops 128 | bytes 1024
  675.4 1.3 while.35
  (138 shorter events, 7.6 us)
Async XLA Ops:
  7.2 95.5 %copy-start = (bf16[2048,3,128]{2,0,1:T(8,128)(2,1)S(1)}, bf16[2048,3,128]{2,0,1:T(8,128)(2,1)}, u32[]{:S(2)}) copy-start(bf16[2048,3,128]{2,0,1:T(8,128)(2,1)} %param.12) | copy-start | bytes 4718596
  7.2 3.8 copy-start.8
  7.2 93.2 %all-gather.4.cloned.1.call-start = ((), (), s32[]{:S(2)}) async-start(), calls=%async_computation.2 | async-start | bytes 2228224 | tf_op jit(solution)/shard_map/all_gather | solution.py:77
  7.9 276.6 %reduce-scatter.4.cloned.1.call-start = ((), (), s32[]{:S(2)}) async-start(), calls=%async_computation.3 | async-start | bytes 2228224
  100.4 2.2 copy-start.1
  103.9 0.9 copy-start.2
  162.0 3.3 copy-start.5
  171.2 114.3 %copy-start.4 = (bf16[512,128]{1,0:T(8,128)(2,1)S(1)}, bf16[512,128]{1,0:T(8,128)(2,1)}, u32[]{:S(2)}) copy-start(bf16[512,128]{1,0:T(8,128)(2,1)} %param.11) | copy-start | bytes 393220
  171.2 120.0 %copy-start.9 = (bf16[128]{0:T(256)(128)(2,1)S(1)}, bf16[128]{0:T(256)(128)(2,1)}, u32[]{:S(2)}) copy-start(bf16[128]{0:T(256)(128)(2,1)} %param.16) | copy-start | bytes 772
  171.2 132.5 %copy-start.3 = (bf16[2376,128]{1,0:T(8,128)(2,1)S(1)}, bf16[2376,128]{1,0:T(8,128)(2,1)}, u32[]{:S(2)}) copy-start(bf16[2376,128]{1,0:T(8,128)(2,1)} %param.17) | copy-start | bytes 1824772
  171.2 137.4 %slice-start = ((bf16[512,3,128]{2,0,1:T(8,128)(2,1)}), bf16[512,2,128]{2,0,1:T(8,128)(2,1)S(1)}, s32[]{:S(2)}) async-start(bf16[512,3,128]{2,0,1:T(8,128)(2,1)} %copy-done.2), calls=%async_computation.5 | async-start | bytes 524288 | tf_op jit(solution)/shard_map/slice | solution.py:89
  285.6 391.6 %copy-start.6 = (bf16[512,128]{1,0:T(8,128)(2,1)}, bf16[512,128]{1,0:T(8,128)(2,1)S(1)}, u32[]{:S(2)}) copy-start(bf16[512,128]{1,0:T(8,128)(2,1)S(1)} %add_convert_fusion) | copy-start | bytes 393220
  286.3 17.4 %all-to-all-start = ((bf16[32,1,128]{2,1,0:T(2,128)(2,1)}), bf16[32,1,128]{2,1,0:T(2,128)(2,1)S(1)}, u32[]{:S(2)}, u32[]{:S(2)}) async-start(bf16[32,1,128]{2,1,0:T(2,128)(2,1)} %stack.2), calls=%async_computation | async-start | bytes 32768 | tf_op jit(solution)/shard_map/all_to_all | solution.py:106
  291.2 259.9 %all-reduce.7.cloned.1.call-start = ((), (), s32[]{:S(2)}) async-start(), calls=%async_computation.4 | async-start | bytes 622592
  676.7 0.5 copy-start.7
Sparse Core Ops, SparseCore 0:
  11.2 89.1 all-gather.3
  171.4 113.0 reduce-scatter.3
  304.9 246.1 all-reduce.6
